TPU v7x, 256 devices: a whole 4x4x8 slice. The times are simulated.
256 devices in a mesh: row: 16 (over y, x_lo, core), col: 16 (over x_hi, z).
Axes of the slice: x: 4 (x_hi: 2, x_lo: 2; x = x_hi * 2 + x_lo), y: 4, z: 8, core: 2. Of those that a mesh axis runs over, the one named last changes fastest.
Arguments:
- w_cycle: float32 [2048, 16384], P('col', 'row'), may hold values from -0.125 to 0.125
- amps: float32 [32, 512, 2048], P('col', 'row'), may hold values from -18 to 18
- eps_occ: float32 [32], replicated, may hold values from -3 to -0.3
- eps_vir: float32 [512], replicated, may hold values from 0.3 to 3
- occ_map: int32 [4], replicated, may hold values from 0 to 31
- vir_perm: int32 [512], replicated, may hold values from 0 to 511, each once
Outputs:
- cycle: float32 [16384, 16384], P('row', 'col')
Inputs may be any that keep to these rules, and one draw needn't show every extreme that they name: `occ_map`: each window index names one occupied orbital. `vir_perm`: each virtual orbital appears once.
All inputs are finite; a program needn't handle non-finite values.
Results may differ from a plain program's by a relative error of at most 0.000071.
Values sent between devices are 32-bit elements; how exact they have to be, the bound alone decides.
No kernel may reach another device: no remote copies, remote signals or barrier semaphores. Data moves between devices by JAX's collectives and lax.ppermute only.
A program may use at most 64 MiB of HBM per device.

v0:
```python
import jax
import jax.numpy as jnp
from jax import lax
from jax.sharding import PartitionSpec as P


def lookup(indices, table):
    onehot = (indices[:, None] == jnp.arange(table.shape[0], dtype=jnp.int32)[None, :]).astype(
        jnp.float32
    )
    return jnp.dot(
        onehot, table, precision=lax.Precision.HIGHEST, preferred_element_type=jnp.float32
    )


def body(w_cycle, amps, eps_occ, eps_vir, occ_map, vir_perm):
    virtual_count = eps_vir.shape[0]
    j_local = amps.shape[0]
    b_local = amps.shape[1]
    vir_energy = lookup(vir_perm, eps_vir)
    occ_energy = lookup(occ_map, eps_occ)
    pair_energy = (vir_energy[None, :] - occ_energy[:, None]).reshape(-1)
    j_index = jnp.arange(j_local, dtype=jnp.int32) + lax.axis_index("col") * j_local
    j_energy = lookup(j_index, eps_occ)
    b_energy = lax.dynamic_slice_in_dim(vir_energy, lax.axis_index("row") * b_local, b_local)
    denominator = pair_energy[None, None, :] + b_energy[None, :, None] - j_energy[:, None, None]
    scaled = amps / denominator
    w_whole = lax.all_gather(w_cycle, "col", axis=0, tiled=True)
    regrouped = lax.all_to_all(scaled, "row", split_axis=2, concat_axis=1, tiled=True)
    t_columns = regrouped.reshape(j_local * virtual_count, regrouped.shape[2])
    return lax.dot_general(
        w_whole,
        lax.all_gather(t_columns, "row", axis=1, tiled=True),
        (((0,), (1,)), ((), ())),
        precision=lax.Precision.HIGHEST,
        preferred_element_type=jnp.float32,
    )


def solution(mesh):
    placed = (P("col", "row"), P("col", "row", None), P(), P(), P(), P())
    return jax.shard_map(
        body, mesh=mesh, in_specs=placed, out_specs=P("row", "col"), check_vma=False
    )
```

profile of v0, /device:TPU:1, one launch (start us, length us, event | category | flops | bytes accessed | tf_op | source)
XLA Modules:
  0.0 258.2 jit_solution(9936301855552644138)
XLA Ops:
  6.5 0.0 copy-start
  6.5 0.0 all-gather.5.cloned.1.call-start
  6.5 0.7 all-gather.5.cloned.1.call-update
  7.3 0.0 all-gather.3.cloned.1.call-start
  7.3 0.0 copy-done
  7.3 1.3 fusion
  8.6 0.1 dynamic_slice.3
  8.7 0.9 convolution_bitcast_fusion.2
  9.6 0.1 subtract_bitcast_fusion
  9.7 0.8 convolution_bitcast_fusion.1
  10.5 0.1 broadcast_add_fusion
  10.6 1.2 subtract_divide_fusion
  11.8 1.0 copy.17
  12.9 2.1 reshape.65
  14.9 16.8 %all_to_all.15 = f32[16,1,8192]{2,1,0:T(1,128)S(1)} all-to-all(f32[16,1,8192]{2,1,0:T(1,128)S(1)} %reshape.65), channel_id=1, replica_groups=mesh['row'=16,'col'=16] {'row'}, dimensions={0} | all-to-all | bytes 1048576 | tf_op jit(solution)/shard_map/all_to_all | solution.py:29
  31.8 0.5 broadcast.35
  32.3 1.9 reduce
  34.2 1.8 reshape.66
  36.0 2.0 copy.22
  37.9 0.0 all-gather.3.cloned.1.call-update
  38.0 113.0 %all-gather.5.cloned.1.call-done = f32[2048,1024]{1,0:T(8,128)} async-done(((f32[128,1024]{1,0:T(8,128)}), f32[2048,1024]{1,0:T(8,128)}) %all-gather.5.cloned.1.call-update) | async-done | bytes 8388624 | tf_op jit(solution)/shard_map/all_gather | solution.py:28
  150.9 63.2 %all-gather.3.cloned.1.call-done = f32[1024,2048]{1,0:T(8,128)} async-done(((f32[1024,128]{1,0:T(8,128)}), f32[1024,2048]{1,0:T(8,128)}) %all-gather.3.cloned.1.call-update) | async-done | bytes 8388624 | tf_op jit(solution)/shard_map/all_gather | solution.py:33
  214.2 31.9 %convolution_bitcast_fusion = f32[1024,1024]{0,1:T(8,128)} fusion(f32[1024,2048]{1,0:T(8,128)} %all-gather.3.cloned.1.call-done, f32[2048,1024]{1,0:T(8,128)} %all-gather.5.cloned.1.call-done), kind=kOutput, calls=%fused_computation | convolution fusion | flops 25769803776 | bytes 20971520 | tf_op jit(solution)/shard_map/dot_general | solution.py:31
  246.0 5.3 %copy.20 = f32[1024,1024]{1,0:T(8,128)} copy(f32[1024,1024]{0,1:T(8,128)} %convolution_bitcast_fusion) | data formatting | bytes 8388608 | tf_op jit(solution)/shard_map/dot_general | solution.py:31
  (2 shorter events, 0.0 us)
Async XLA Ops:
  6.5 0.8 copy-start
  6.5 144.4 %all-gather.5.cloned.1.call-start = ((), (), s32[]{:S(2)}) async-start(), calls=%async_computation.2 | async-start | bytes 8912896 | tf_op jit(solution)/shard_map/all_gather | solution.py:28
  7.3 206.9 %all-gather.3.cloned.1.call-start = ((), (), s32[]{:S(2)}) async-start(), calls=%async_computation.1 | async-start | bytes 8912896 | tf_op jit(solution)/shard_map/all_gather | solution.py:33
Sparse Core Ops, SparseCore 0:
  9.9 140.9 all-gather.4
  152.7 61.4 all-gather.2
where the time goes:
time: 258 us
  waiting for transfers between devices  177 us (69%)
  matrix products  34.9 us (14%)
  blocking collectives  16.8 us (7%)
  between operations  13.5 us (5%)
  local copies, waits for them, and re-layouts  12.8 us (5%)
  other arithmetic  3.28 us (1%)
    all_gather x1, waiting for transfers between devices, body(): w_whole = lax.all_gather(w_cycle, 'col', axis=0, tiled=True)  113 us
    all_gather x1, waiting for transfers between devices, body(): lax.all_gather(t_columns, 'row', axis=1, tiled=True)  63.2 us
    dot_general x1, matrix products, body(): lax.dot_general(w_whole, lax.all_gather(t_columns, 'row', axis=1, tiled=T...  31.9 us
    all_to_all x1, blocking collectives, body(): lax.all_to_all(scaled, 'row', split_axis=2, concat_axis=1, tiled=True)  16.8 us
    dot_general x1, local copies, waits for them, and re-layouts, body(): lax.dot_general(w_whole, lax.all_gather(t_columns, 'row', axis=1, tiled=T...  5.34 us
  transfers between devices with their start and end apart: 2, of which 2 were waited for; matrix products, arithmetic and copies ran while one was open for 5% of the time, Pallas kernels for 0%

commit v1 on v0

--- a/solution.py
+++ b/solution.py
@@ -2,6 +2,19 @@
 import jax.numpy as jnp
 from jax import lax
 from jax.sharding import PartitionSpec as P
+
+
+def _expand_widths(raw):
+    clean = jnp.concatenate(
+        lax.all_to_all(
+            jnp.stack([raw for _ in range(lax.axis_size("row"))], axis=0),
+            "row",
+            split_axis=0,
+            concat_axis=0,
+        ),
+        axis=1,
+    )
+    return clean
 
 
 def lookup(indices, table):
@@ -30,7 +43,7 @@
     t_columns = regrouped.reshape(j_local * virtual_count, regrouped.shape[2])
     return lax.dot_general(
         w_whole,
-        lax.all_gather(t_columns, "row", axis=1, tiled=True),
+        _expand_widths(t_columns),
         (((0,), (1,)), ((), ())),
         precision=lax.Precision.HIGHEST,
         preferred_element_type=jnp.float32,

time: 258 us -> 240 us (0.930)
  waiting for transfers between devices: 177 us -> 14.7 us
  blocking collectives: 16.8 us -> 161 us
    all_to_all x0 -> x1, blocking collectives: none -> 144 us  [_expand_widths(): lax.all_to_all(jnp.stack([raw for _ in range(lax.axis_size('row'))], axis...]
    all_gather x1, waiting for transfers between devices: 113 us -> 14 us  [body(): w_whole = lax.all_gather(w_cycle, 'col', axis=0, tiled=True)]
    all_gather x1 -> x0, waiting for transfers between devices: 63.2 us -> none  [body(): lax.all_gather(t_columns, 'row', axis=1, tiled=True)]
  transfers between devices with their start and end apart: 2 -> 1, of which waited for: 2 -> 1; matrix products, arithmetic and copies ran while one was open for 5% -> 6% of each run, Pallas kernels for 0% -> 0%
where the time goes in v1:
time: 240 us
  blocking collectives  161 us (67%)
  matrix products  34.7 us (14%)
  waiting for transfers between devices  14.7 us (6%)
  between operations  13.5 us (6%)
  local copies, waits for them, and re-layouts  13 us (5%)
  other arithmetic  3.28 us (1%)
    all_to_all x1, blocking collectives, _expand_widths(): lax.all_to_all(jnp.stack([raw for _ in range(lax.axis_size('row'))], axis...  144 us
    dot_general x1, matrix products, body(): lax.dot_general(w_whole, _expand_widths(t_columns), (((0,), (1,)), ((), (...  31.6 us
    all_to_all x1, blocking collectives, body(): lax.all_to_all(scaled, 'row', split_axis=2, concat_axis=1, tiled=True)  16.8 us
    all_gather x1, waiting for transfers between devices, body(): w_whole = lax.all_gather(w_cycle, 'col', axis=0, tiled=True)  14 us
    dot_general x1, local copies, waits for them, and re-layouts, body(): lax.dot_general(w_whole, _expand_widths(t_columns), (((0,), (1,)), ((), (...  5.34 us
  transfers between devices with their start and end apart: 1, of which 1 were waited for; matrix products, arithmetic and copies ran while one was open for 6% of the time, Pallas kernels for 0%

profile of v1, /device:TPU:1, one launch (start us, length us, event | category | flops | bytes accessed | tf_op | source)
XLA Modules:
  0.0 240.2 jit_solution(7007472429179077650)
XLA Ops:
  6.5 0.0 copy-start
  6.5 0.0 all-gather.2.cloned.1.call-start
  6.5 0.7 all-gather.2.cloned.1.call-update
  7.3 0.0 copy-done
  7.3 1.3 fusion
  8.6 0.1 dynamic_slice.3
  8.7 0.9 convolution_bitcast_fusion.2
  9.5 0.1 subtract_bitcast_fusion
  9.6 0.8 convolution_bitcast_fusion.1
  10.5 0.1 broadcast_add_fusion
  10.6 1.2 subtract_divide_fusion
  11.8 1.0 copy.20
  12.8 2.1 reshape.71
  14.9 16.8 %all_to_all.20 = f32[16,1,8192]{2,1,0:T(1,128)S(1)} all-to-all(f32[16,1,8192]{2,1,0:T(1,128)S(1)} %reshape.71), channel_id=1, replica_groups=mesh['row'=16,'col'=16] {'row'}, dimensions={0} | all-to-all | bytes 1048576 | tf_op jit(solution)/shard_map/all_to_all | solution.py:42
  31.7 0.5 broadcast.36
  32.2 1.9 reduce
  34.1 1.8 reshape.72
  35.9 0.9 copy.26
  36.8 0.2 copy.23
  37.0 1.1 stack.3
  38.1 144.3 %all_to_all.21 = f32[16,1024,128]{1,2,0:T(8,128)} all-to-all(f32[16,1024,128]{1,2,0:T(8,128)S(1)} %stack.3), channel_id=1, replica_groups=mesh['row'=16,'col'=16] {'row'}, dimensions={0} | all-to-all | bytes 16777216 | tf_op jit(solution)/shard_map/all_to_all | solution.py:9
  182.3 14.0 %all-gather.2.cloned.1.call-done = f32[2048,1024]{1,0:T(8,128)} async-done(((f32[128,1024]{1,0:T(8,128)}), f32[2048,1024]{1,0:T(8,128)}) %all-gather.2.cloned.1.call-update) | async-done | bytes 8388624 | tf_op jit(solution)/shard_map/all_gather | solution.py:41
  196.3 31.6 %convolution_bitcast_fusion = f32[1024,1024]{0,1:T(8,128)} fusion(f32[1024,2048]{0,1:T(8,128)} %bitcast.33, f32[2048,1024]{1,0:T(8,128)} %all-gather.2.cloned.1.call-done), kind=kOutput, calls=%fused_computation | convolution fusion | flops 25769803776 | bytes 20971520 | tf_op jit(solution)/shard_map/dot_general | solution.py:44
  228.0 5.3 %copy.24 = f32[1024,1024]{1,0:T(8,128)} copy(f32[1024,1024]{0,1:T(8,128)} %convolution_bitcast_fusion) | data formatting | bytes 8388608 | tf_op jit(solution)/shard_map/dot_general | solution.py:44
  (2 shorter events, 0.0 us)
Async XLA Ops:
  6.5 0.7 copy-start
  6.5 189.8 %all-gather.2.cloned.1.call-start = ((), (), s32[]{:S(2)}) async-start(), calls=%async_computation.2 | async-start | bytes 8912896 | tf_op jit(solution)/shard_map/all_gather | solution.py:41
Sparse Core Ops, SparseCore 0:
  9.9 186.3 all-gather.1

commit v2 on v0

--- a/solution.py
+++ b/solution.py
@@ -2,6 +2,19 @@
 import jax.numpy as jnp
 from jax import lax
 from jax.sharding import PartitionSpec as P
+
+
+def deliver_racks(mine):
+    row_out = jnp.concatenate(
+        jax.lax.all_to_all(
+            jnp.stack(jnp.split(mine, jax.lax.axis_size("row"), 2), 0),
+            axis_name="row",
+            split_axis=0,
+            concat_axis=0,
+        ),
+        1,
+    )
+    return row_out
 
 
 def lookup(indices, table):
@@ -26,7 +39,7 @@
     denominator = pair_energy[None, None, :] + b_energy[None, :, None] - j_energy[:, None, None]
     scaled = amps / denominator
     w_whole = lax.all_gather(w_cycle, "col", axis=0, tiled=True)
-    regrouped = lax.all_to_all(scaled, "row", split_axis=2, concat_axis=1, tiled=True)
+    regrouped = deliver_racks(scaled)
     t_columns = regrouped.reshape(j_local * virtual_count, regrouped.shape[2])
     return lax.dot_general(
         w_whole,

time: 258 us -> 256 us (level)
  local copies, waits for them, and re-layouts: 12.8 us -> 6.37 us
  waiting for transfers between devices: 177 us -> 183 us
    all_gather x1, waiting for transfers between devices: 113 us -> 119 us  [body(): w_whole = lax.all_gather(w_cycle, 'col', axis=0, tiled=True)]
    unnamed x5 -> x18, local copies, waits for them, and re-layouts: 3.85 us -> 0.11 us
  transfers between devices with their start and end apart: 2 -> 2, of which waited for: 2 -> 2; matrix products, arithmetic and copies ran while one was open for 5% -> 2% of each run, Pallas kernels for 0% -> 0%
where the time goes in v2:
time: 256 us; the launch traced here: 255 us
  waiting for transfers between devices  183 us (71%)
  matrix products  34.9 us (14%)
  blocking collectives  16.4 us (6%)
  between operations  13.6 us (5%)
  local copies, waits for them, and re-layouts  6.37 us (2%)
    all_gather x1, waiting for transfers between devices, body(): w_whole = lax.all_gather(w_cycle, 'col', axis=0, tiled=True)  119 us
    all_gather x1, waiting for transfers between devices, body(): lax.all_gather(t_columns, 'row', axis=1, tiled=True)  63.2 us
    dot_general x1, matrix products, body(): lax.dot_general(w_whole, lax.all_gather(t_columns, 'row', axis=1, tiled=T...  31.9 us
    all_to_all x1, blocking collectives, deliver_racks(): jax.lax.all_to_all(jnp.stack(jnp.split(mine, jax.lax.axis_size('row'), 2)...  16.4 us
    dot_general x1, local copies, waits for them, and re-layouts, body(): lax.dot_general(w_whole, lax.all_gather(t_columns, 'row', axis=1, tiled=T...  5.34 us
  transfers between devices with their start and end apart: 2, of which 2 were waited for; matrix products, arithmetic and copies ran while one was open for 2% of the time, Pallas kernels for 0%

profile of v2, /device:TPU:1, one launch (start us, length us, event | category | flops | bytes accessed | tf_op | source)
XLA Modules:
  0.0 255.4 jit_solution(11261311295360860019)
XLA Ops:
  6.5 0.0 copy-start
  6.5 0.0 all-gather.5.cloned.1.call-start
  6.5 0.7 all-gather.5.cloned.1.call-update
  7.3 0.0 all-gather.3.cloned.1.call-start
  7.3 0.0 copy-done
  7.3 1.3 fusion
  8.6 0.1 dynamic_slice.3
  8.7 0.9 convolution_bitcast_fusion.2
  9.6 0.1 subtract_bitcast_fusion
  9.7 0.8 convolution_bitcast_fusion.1
  10.5 0.1 broadcast_add_fusion
  10.6 1.2 subtract_divide_fusion
  12.1 16.4 %all_to_all.5 = f32[16,2,32,128]{3,2,1,0:T(8,128)S(1)} all-to-all(f32[16,2,32,128]{3,2,1,0:T(8,128)S(1)} %constant_dynamic-update-slice_fusion), channel_id=1, replica_groups=mesh['row'=16,'col'=16] {'row'}, dimensions={0} | all-to-all | bytes 1048576 | tf_op jit(solution)/shard_map/all_to_all | solution.py:9
  28.4 0.8 copy.24
  29.3 0.0 all-gather.3.cloned.1.call-update
  29.3 118.9 %all-gather.5.cloned.1.call-done = f32[2048,1024]{1,0:T(8,128)} async-done(((f32[128,1024]{1,0:T(8,128)}), f32[2048,1024]{1,0:T(8,128)}) %all-gather.5.cloned.1.call-update) | async-done | bytes 8388624 | tf_op jit(solution)/shard_map/all_gather | solution.py:41
  148.2 63.2 %all-gather.3.cloned.1.call-done = f32[1024,2048]{1,0:T(8,128)} async-done(((f32[1024,128]{1,0:T(8,128)}), f32[1024,2048]{1,0:T(8,128)}) %all-gather.3.cloned.1.call-update) | async-done | bytes 8388624 | tf_op jit(solution)/shard_map/all_gather | solution.py:46
  211.4 31.9 %convolution_bitcast_fusion = f32[1024,1024]{0,1:T(8,128)} fusion(f32[1024,2048]{1,0:T(8,128)} %all-gather.3.cloned.1.call-done, f32[2048,1024]{1,0:T(8,128)} %all-gather.5.cloned.1.call-done), kind=kOutput, calls=%fused_computation | convolution fusion | flops 25769803776 | bytes 20971520 | tf_op jit(solution)/shard_map/dot_general | solution.py:44
  243.3 5.3 %copy.25 = f32[1024,1024]{1,0:T(8,128)} copy(f32[1024,1024]{0,1:T(8,128)} %convolution_bitcast_fusion) | data formatting | bytes 8388608 | tf_op jit(solution)/shard_map/dot_general | solution.py:44
  (18 shorter events, 0.1 us)
Async XLA Ops:
  6.5 0.8 copy-start
  6.5 141.6 %all-gather.5.cloned.1.call-start = ((), (), s32[]{:S(2)}) async-start(), calls=%async_computation.2 | async-start | bytes 8912896 | tf_op jit(solution)/shard_map/all_gather | solution.py:41
  7.3 204.1 %all-gather.3.cloned.1.call-start = ((), (), s32[]{:S(2)}) async-start(), calls=%async_computation.1 | async-start | bytes 8912896 | tf_op jit(solution)/shard_map/all_gather | solution.py:46
Sparse Core Ops, SparseCore 0:
  9.9 138.2 all-gather.4
  149.9 61.4 all-gather.2
